TPU v7x, 512 devices: a whole 4x8x8 slice. The times are simulated.
512 devices in a mesh: pipe: 4 (over z_hi), ctx: 32 (over y, z_lo, core), dp: 4 (over x).
Axes of the slice: x: 4, y: 8, z: 8 (z_hi: 4, z_lo: 2; z = z_hi * 2 + z_lo), core: 2. Of those that a mesh axis runs over, the one named last changes fastest.
Arguments:
- queries: bfloat16 [4, 4, 4096, 4096], P('pipe', 'dp', 'ctx'), may hold values from -7 to 7
- key_input: bfloat16 [4, 4, 4096, 512], P('pipe', 'dp', 'ctx'), may hold values from -4 to 4
- value_input: bfloat16 [4, 4, 4096, 512], P('pipe', 'dp', 'ctx'), may hold values from -6 to 6
- incoming: bfloat16 [4, 4, 4096, 4096], P('pipe', 'dp', 'ctx'), may hold values from -6 to 6
- segments: int32 [4, 4096], P('dp'), may hold values from 0 to 15, never falling along the last dimension, each value on 1 to 512 neighbouring positions
Outputs:
- query_grad: bfloat16 [4, 4, 4096, 4096], P('pipe', 'dp', 'ctx')
- key_grad: bfloat16 [4, 4, 4096, 512], P('pipe', 'dp', 'ctx')
- value_grad: bfloat16 [4, 4, 4096, 512], P('pipe', 'dp', 'ctx')
- bias_grad: float32 [4, 5120], P('pipe')
Inputs may be any that keep to these rules, and one draw needn't show every extreme that they name: `segments`: tokens of one document are contiguous; every document holds 1 to 512 tokens and one holds exactly 512.
All inputs are finite; a program needn't handle non-finite values.
Results may differ from a plain program's by a relative error of at most 0.009.
Values may be sent and summed in bfloat16 or wider, within the bound.
No kernel may reach another device: no remote copies, remote signals or barrier semaphores. Data moves between devices by JAX's collectives and lax.ppermute only.
A program may use at most 64 MiB of HBM per device.

v0:
```python
import math
import jax
import jax.numpy as jnp
from jax import lax
from jax.sharding import PartitionSpec as P

ASKER_STREAMS = 32
SHARED_GROUPS = 4
FEATURE_SIZE = 128
QUERY_PER_KEY = 8


def passed_along(value, axis, steps):
    count = lax.axis_size(axis)
    pairs = [(source, (source + steps) % count) for source in range(count)]
    return lax.ppermute(value, axis, pairs)


def attend(
    queries, key_rows, value_rows, cotangent, query_doc, key_doc, query_pos, key_pos, scaling
):
    scores = (
        jnp.einsum("gqd,kd->gqk", queries, key_rows, preferred_element_type=jnp.float32) * scaling
    )
    visible = (query_doc[:, None] == key_doc[None, :]) & (key_pos[None, :] <= query_pos[:, None])
    scores = jnp.where(visible[None], scores, -1e30)
    row_max = jnp.max(scores, axis=-1, keepdims=True)
    weights = jnp.where(visible[None], jnp.exp(scores - row_max), 0.0)
    probs = weights / jnp.sum(weights, axis=-1, keepdims=True)
    probs_b = probs.astype(jnp.bfloat16)
    attn_out = jnp.einsum("gqk,kd->gqd", probs_b, value_rows, preferred_element_type=jnp.float32)
    dot_out = jnp.sum(cotangent.astype(jnp.float32) * attn_out, axis=-1, keepdims=True)
    grad_prob = jnp.einsum("gqd,kd->gqk", cotangent, value_rows, preferred_element_type=jnp.float32)
    grad_score = (probs * (grad_prob - dot_out) * scaling).astype(jnp.bfloat16)
    asker_derivative = jnp.einsum(
        "gqk,kd->gqd", grad_score, key_rows, preferred_element_type=jnp.float32
    )
    lookup_derivative = jnp.einsum(
        "gqk,gqd->kd", grad_score, queries, preferred_element_type=jnp.float32
    )
    content_derivative = jnp.einsum(
        "gqk,gqd->kd", probs_b, cotangent, preferred_element_type=jnp.float32
    )
    return (asker_derivative, lookup_derivative, content_derivative)


def banded(queries, key_rows, value_rows, cotangent, doc_ids, block_len, scaling):
    length = doc_ids.shape[0]
    blocks = length // block_len
    width = key_rows.shape[1]
    key_pad = jnp.concatenate([jnp.zeros((block_len, width), key_rows.dtype), key_rows], axis=0)
    value_pad = jnp.concatenate(
        [jnp.zeros((block_len, width), value_rows.dtype), value_rows], axis=0
    )
    doc_pad = jnp.concatenate([jnp.full((block_len,), -1, jnp.int32), doc_ids])
    pos_pad = jnp.arange(length + block_len, dtype=jnp.int32) - block_len

    def step(carried, block):
        key_acc, value_acc = carried
        anchor = block * block_len
        query_blk = lax.dynamic_slice_in_dim(queries, anchor, block_len, 1)
        cot_blk = lax.dynamic_slice_in_dim(cotangent, anchor, block_len, 1)
        key_blk = lax.dynamic_slice_in_dim(key_pad, anchor, 2 * block_len, 0)
        value_blk = lax.dynamic_slice_in_dim(value_pad, anchor, 2 * block_len, 0)
        query_doc = lax.dynamic_slice_in_dim(doc_ids, anchor, block_len, 0)
        key_doc = lax.dynamic_slice_in_dim(doc_pad, anchor, 2 * block_len, 0)
        query_pos = anchor + jnp.arange(block_len, dtype=jnp.int32)
        key_pos = lax.dynamic_slice_in_dim(pos_pad, anchor, 2 * block_len, 0)
        asker_derivative, lookup_derivative, content_derivative = attend(
            query_blk, key_blk, value_blk, cot_blk, query_doc, key_doc, query_pos, key_pos, scaling
        )
        key_acc = lax.dynamic_update_slice_in_dim(
            key_acc,
            lax.dynamic_slice_in_dim(key_acc, anchor, 2 * block_len, 0) + lookup_derivative,
            anchor,
            0,
        )
        value_acc = lax.dynamic_update_slice_in_dim(
            value_acc,
            lax.dynamic_slice_in_dim(value_acc, anchor, 2 * block_len, 0) + content_derivative,
            anchor,
            0,
        )
        return ((key_acc, value_acc), asker_derivative)

    start_acc = jnp.zeros((length + block_len, width), jnp.float32)
    (key_acc, value_acc), query_blocks = lax.scan(
        step, (start_acc, start_acc), jnp.arange(blocks, dtype=jnp.int32)
    )
    groups = queries.shape[0]
    asker_derivative = query_blocks.transpose(1, 0, 2, 3).reshape(groups, length, width)
    return (asker_derivative, key_acc[block_len:], value_acc[block_len:])


def body(queries, key_input, value_input, incoming, segments):
    shard_length = queries.shape[2]
    ctx_size = lax.axis_size("ctx")
    reach_dev = min(4, ctx_size - 1)
    block_len = reach_dev * shard_length
    scaling = 1.0 / math.sqrt(FEATURE_SIZE)
    doc_ids = segments[0]
    handed = passed_along(incoming, "pipe", -1)
    query_tok = queries[0, 0].reshape(shard_length, ASKER_STREAMS, FEATURE_SIZE)
    cot_tok = handed[0, 0].reshape(shard_length, ASKER_STREAMS, FEATURE_SIZE)
    key_widened = jnp.repeat(
        key_input[0, 0].reshape(shard_length, SHARED_GROUPS, FEATURE_SIZE), QUERY_PER_KEY, axis=1
    )
    value_widened = jnp.repeat(
        value_input[0, 0].reshape(shard_length, SHARED_GROUPS, FEATURE_SIZE), QUERY_PER_KEY, axis=1
    )
    query_head, key_head, value_head, cot_head = (
        lax.all_to_all(query_tok, "ctx", split_axis=1, concat_axis=0, tiled=True),
        lax.all_to_all(key_widened, "ctx", split_axis=1, concat_axis=0, tiled=True),
        lax.all_to_all(value_widened, "ctx", split_axis=1, concat_axis=0, tiled=True),
        lax.all_to_all(cot_tok, "ctx", split_axis=1, concat_axis=0, tiled=True),
    )

    def per_head(members):
        return banded(
            members[0][None], members[1], members[2], members[3][None], doc_ids, block_len, scaling
        )

    asker_derivative, lookup_derivative, content_derivative = lax.map(
        per_head,
        (
            query_head.transpose(1, 0, 2),
            key_head.transpose(1, 0, 2),
            value_head.transpose(1, 0, 2),
            cot_head.transpose(1, 0, 2),
        ),
    )
    asker_derivative = asker_derivative[:, 0].transpose(1, 0, 2)
    lookup_derivative = lookup_derivative.transpose(1, 0, 2)
    content_derivative = content_derivative.transpose(1, 0, 2)
    query_back, key_backward, value_backward = (
        lax.all_to_all(asker_derivative, "ctx", split_axis=0, concat_axis=1, tiled=True),
        lax.all_to_all(lookup_derivative, "ctx", split_axis=0, concat_axis=1, tiled=True),
        lax.all_to_all(content_derivative, "ctx", split_axis=0, concat_axis=1, tiled=True),
    )
    query_flat = query_back.reshape(shard_length, ASKER_STREAMS * FEATURE_SIZE)
    key_flattened = (
        key_backward.reshape(shard_length, SHARED_GROUPS, QUERY_PER_KEY, FEATURE_SIZE)
        .sum(axis=2)
        .reshape(shard_length, SHARED_GROUPS * FEATURE_SIZE)
    )
    value_flat = (
        value_backward.reshape(shard_length, SHARED_GROUPS, QUERY_PER_KEY, FEATURE_SIZE)
        .sum(axis=2)
        .reshape(shard_length, SHARED_GROUPS * FEATURE_SIZE)
    )
    offset_parts = jnp.concatenate(
        [jnp.sum(query_flat, axis=0), jnp.sum(key_flattened, axis=0), jnp.sum(value_flat, axis=0)]
    )
    offset_overall = lax.psum(offset_parts, ("ctx", "dp"))
    bias_scaled = offset_overall / math.sqrt(lax.axis_size("dp") * shard_length * ctx_size)
    query_grad = query_flat.astype(jnp.bfloat16)[None, None]
    key_grad = key_flattened.astype(jnp.bfloat16)[None, None]
    value_grad = value_flat.astype(jnp.bfloat16)[None, None]
    return (query_grad, key_grad, value_grad, bias_scaled[None])


def solution(mesh):
    return jax.shard_map(
        body,
        mesh=mesh,
        in_specs=(
            P("pipe", "dp", "ctx", None),
            P("pipe", "dp", "ctx", None),
            P("pipe", "dp", "ctx", None),
            P("pipe", "dp", "ctx", None),
            P("dp", None),
        ),
        out_specs=(
            P("pipe", "dp", "ctx", None),
            P("pipe", "dp", "ctx", None),
            P("pipe", "dp", "ctx", None),
            P("pipe", None),
        ),
        check_vma=False,
    )
```

profile of v0, /device:TPU:128, one launch (start us, length us, event | category | flops | bytes accessed | tf_op | source)
XLA Modules:
  0.0 1042.6 jit_solution(12610844461914456718)
XLA Ops:
  2.9 9.3 all-to-all-start.1
  12.2 28.5 %all-to-all-done.1 = bf16[128,32,128]{2,0,1:T(8,128)(2,1)S(1)} async-done(((bf16[128,32,128]{2,0,1:T(8,128)(2,1)}), bf16[128,32,128]{2,0,1:T(8,128)(2,1)S(1)}, u32[]{:S(2)}, u32[]{:S(2)}) %all-to-all-start.1) | async-done | bytes 1048608 | tf_op jit(solution)/shard_map/all_to_all | solution.py:113
  42.0 3.9 all-to-all-start.3
  47.8 37.3 %collective-permute-done = bf16[1,1,128,4096]{3,2,1,0:T(8,128)(2,1)S(1)} collective-permute-done((bf16[1,1,128,4096]{3,2,1,0:T(8,128)(2,1)}, bf16[1,1,128,4096]{3,2,1,0:T(8,128)(2,1)S(1)}, u32[]{:S(2)}, u32[]{:S(2)}) %collective-permute-start) | collective-permute-done | bytes 1048608 | tf_op jit(solution)/shard_map/ppermute | solution.py:16
  86.5 30.7 %all-to-all-start.2 = ((bf16[128,32,128]{0,2,1:T(8,128)(2,1)}), bf16[128,32,128]{0,2,1:T(8,128)(2,1)S(1)}, u32[]{:S(2)}, u32[]{:S(2)}) async-start(bf16[128,32,128]{0,2,1:T(8,128)(2,1)} %bitcast.112), calls=%async_computation.2 | async-start | bytes 2097152 | tf_op jit(solution)/shard_map/all_to_all | solution.py:115
  120.1 25.7 %all-to-all-done.2 = bf16[128,32,128]{0,2,1:T(8,128)(2,1)S(1)} async-done(((bf16[128,32,128]{0,2,1:T(8,128)(2,1)}), bf16[128,32,128]{0,2,1:T(8,128)(2,1)S(1)}, u32[]{:S(2)}, u32[]{:S(2)}) %all-to-all-start.2) | async-done | bytes 1048608 | tf_op jit(solution)/shard_map/all_to_all | solution.py:115
  145.8 4.7 all-to-all-start
  154.3 25.3 %all-to-all-done = bf16[128,32,128]{2,0,1:T(8,128)(2,1)} async-done(((bf16[128,32,128]{2,0,1:T(8,128)(2,1)}), bf16[128,32,128]{2,0,1:T(8,128)(2,1)}, u32[]{:S(2)}, u32[]{:S(2)}) %all-to-all-start) | async-done | bytes 1048608 | tf_op jit(solution)/shard_map/all_to_all | solution.py:112
  183.3 126.4 %while.25 = (s32[]{:T(128)}, f32[4608,128]{1,0:T(8,128)}, f32[4608,128]{1,0:T(8,128)}, f32[8,1,512,128]{3,2,1,0:T(8,128)}, s32[8]{0:T(128)}, /*index=5*/s32[4096...) while((s32[]{:T(128)}, f32[4608,128]{1,0:T(8,128)}, ...), condition=%wide.region_4.5_spmd, body=%wide.region_0.4_spmd.sunk | while | flops 820444160 | bytes 22487844 | solution.py:87
  208.1 2.4 fusion.59
  223.9 2.4 fusion.59
  239.7 2.4 fusion.59
  255.5 2.4 fusion.59
  271.3 2.4 fusion.59
  287.1 2.4 fusion.59
  302.9 2.4 fusion.59
  309.7 3.1 slice.8
  312.8 4.0 all-to-all-start.5
  316.8 3.1 slice.9
  319.9 48.6 %all-to-all-done.5 = f32[4096,1,128]{2,1,0:T(1,128)S(1)} async-done(((f32[4096,1,128]{2,1,0:T(1,128)}), f32[4096,1,128]{2,1,0:T(1,128)S(1)}, u32[]{:S(2)}, u32[]{:S(2)}) %all-to-all-start.5) | async-done | bytes 2097184 | tf_op jit(solution)/shard_map/all_to_all | solution.py:137
  368.5 56.4 %all_to_all.105 = f32[4096,1,128]{2,1,0:T(1,128)} all-to-all(f32[4096,1,128]{2,1,0:T(1,128)} %bitcast.109), channel_id=1, replica_groups=mesh['pipe'=4,'ctx'=32,'dp'=4] {'ctx'}, dimensions={0} | all-to-all | bytes 4194304 | tf_op jit(solution)/shard_map/all_to_all | solution.py:138
  424.9 4.8 all-to-all-start.4
  431.6 49.7 %all-to-all-done.4 = f32[4096,1,128]{2,1,0:T(1,128)} async-done(((f32[4096,1,128]{2,1,0:T(1,128)}), f32[4096,1,128]{2,1,0:T(1,128)}, u32[]{:S(2)}, u32[]{:S(2)}) %all-to-all-start.4) | async-done | bytes 2097184 | tf_op jit(solution)/shard_map/all_to_all | solution.py:136
  484.8 549.9 %psum.7 = f32[5120]{0:T(1024)S(1)} all-reduce(f32[5120]{0:T(1024)S(1)} %pad_maximum_fusion), channel_id=1, replica_groups=mesh['pipe'=4,'ctx'=32,'dp'=4] {'ctx','dp'}, use_global_device_ids=true, to_apply=%region_12.13 | all-reduce | flops 5120 | bytes 40960 | tf_op jit(solution)/shard_map/psum | solution.py:154
  (153 shorter events, 135.0 us)
Async XLA Ops:
  0.6 11.5 %copy-start = (bf16[1,1,128,512]{3,2,1,0:T(8,128)(2,1)S(1)}, bf16[1,1,128,512]{3,2,1,0:T(8,128)(2,1)}, u32[]{:S(2)}) copy-start(bf16[1,1,128,512]{3,2,1,0:T(8,128)(2,1)} %param.9) | copy-start | bytes 393220
  2.9 37.9 %all-to-all-start.1 = ((bf16[128,32,128]{2,0,1:T(8,128)(2,1)}), bf16[128,32,128]{2,0,1:T(8,128)(2,1)S(1)}, u32[]{:S(2)}, u32[]{:S(2)}) async-start(bf16[128,32,128]{2,0,1:T(8,128)(2,1)} %bitcast.9), calls=%async_computation.1 | async-start | bytes 2097152 | tf_op jit(solution)/shard_map/all_to_all | solution.py:113
  42.0 44.5 %all-to-all-start.3 = ((bf16[128,32,128]{2,0,1:T(8,128)(2,1)}), bf16[128,32,128]{2,0,1:T(8,128)(2,1)S(1)}, u32[]{:S(2)}, u32[]{:S(2)}) async-start(bf16[128,32,128]{2,0,1:T(8,128)(2,1)} %bitcast.17), calls=%async_computation.3 | async-start | bytes 2097152 | tf_op jit(solution)/shard_map/all_to_all | solution.py:114
  45.9 39.3 %collective-permute-start = (bf16[1,1,128,4096]{3,2,1,0:T(8,128)(2,1)}, bf16[1,1,128,4096]{3,2,1,0:T(8,128)(2,1)S(1)}, u32[]{:S(2)}, u32[]{:S(2)}) collective-permute-start(bf16[1,1,128,4096]{3,2,1,0:T(8,128)(2,1)} %param.10), channel_id=1, source_target_pairs={{0,384},{128,0},{256,128},{384,256},{1,385},{129,1},{257,129},{385... | collective-permute-start | bytes 3145736 | tf_op jit(solution)/shard_map/ppermute | solution.py:16
  86.5 59.3 %all-to-all-start.2 = ((bf16[128,32,128]{0,2,1:T(8,128)(2,1)}), bf16[128,32,128]{0,2,1:T(8,128)(2,1)S(1)}, u32[]{:S(2)}, u32[]{:S(2)}) async-start(bf16[128,32,128]{0,2,1:T(8,128)(2,1)} %bitcast.112), calls=%async_computation.2 | async-start | bytes 2097152 | tf_op jit(solution)/shard_map/all_to_all | solution.py:115
  118.7 31.8 %copy-start.1 = (s32[1,4096]{1,0:T(1,128)S(1)}, s32[1,4096]{1,0:T(1,128)}, u32[]{:S(2)}) copy-start(s32[1,4096]{1,0:T(1,128)} %param.11) | copy-start | bytes 49156
  145.8 33.8 %all-to-all-start = ((bf16[128,32,128]{2,0,1:T(8,128)(2,1)}), bf16[128,32,128]{2,0,1:T(8,128)(2,1)}, u32[]{:S(2)}, u32[]{:S(2)}) async-start(bf16[128,32,128]{2,0,1:T(8,128)(2,1)} %copy.41), calls=%async_computation | async-start | bytes 2097152 | tf_op jit(solution)/shard_map/all_to_all | solution.py:112
  312.8 55.7 %all-to-all-start.5 = ((f32[4096,1,128]{2,1,0:T(1,128)}), f32[4096,1,128]{2,1,0:T(1,128)S(1)}, u32[]{:S(2)}, u32[]{:S(2)}) async-start(f32[4096,1,128]{2,1,0:T(1,128)} %bitcast.108), calls=%async_computation.5 | async-start | bytes 4194304 | tf_op jit(solution)/shard_map/all_to_all | solution.py:137
  424.9 56.4 %all-to-all-start.4 = ((f32[4096,1,128]{2,1,0:T(1,128)}), f32[4096,1,128]{2,1,0:T(1,128)}, u32[]{:S(2)}, u32[]{:S(2)}) async-start(f32[4096,1,128]{2,1,0:T(1,128)} %bitcast.116), calls=%async_computation.4 | async-start | bytes 4194304 | tf_op jit(solution)/shard_map/all_to_all | solution.py:136
where the time goes:
time: 1050 us; the launch traced here: 1040 us
  blocking collectives  606 us (58%)
  waiting for transfers between devices  215 us (20%)
  matrix products  76.1 us (7%)
  starting transfers between devices  59.3 us (6%)
  local copies, waits for them, and re-layouts  57 us (5%)
  other arithmetic  23 us (2%)
    psum x1, blocking collectives, body(): offset_overall = lax.psum(offset_parts, ('ctx', 'dp'))  550 us
    all_to_all x1, blocking collectives, body(): lax.all_to_all(content_derivative, 'ctx', split_axis=0, concat_axis=1, ti...  56.4 us
    all_to_all x1, waiting for transfers between devices, body(): lax.all_to_all(asker_derivative, 'ctx', split_axis=0, concat_axis=1, tile...  49.7 us
    all_to_all x1, waiting for transfers between devices, body(): lax.all_to_all(lookup_derivative, 'ctx', split_axis=0, concat_axis=1, til...  48.6 us
    ppermute x1, waiting for transfers between devices, passed_along(): return lax.ppermute(value, axis, pairs)  37.3 us
    all_to_all x1, starting transfers between devices, body(): lax.all_to_all(cot_tok, 'ctx', split_axis=1, concat_axis=0, tiled=True)  30.7 us
    all_to_all x1, waiting for transfers between devices, body(): lax.all_to_all(key_widened, 'ctx', split_axis=1, concat_axis=0, tiled=True)  28.5 us
    all_to_all x1, waiting for transfers between devices, body(): lax.all_to_all(cot_tok, 'ctx', split_axis=1, concat_axis=0, tiled=True)  25.7 us
  transfers between devices with their start and end apart: 7, of which 6 were waited for; matrix products, arithmetic and copies ran while one was open for 1% of the time, Pallas kernels for 0%

commit v1 on v0

--- a/solution.py
+++ b/solution.py
@@ -151,7 +151,8 @@
     offset_parts = jnp.concatenate(
         [jnp.sum(query_flat, axis=0), jnp.sum(key_flattened, axis=0), jnp.sum(value_flat, axis=0)]
     )
-    offset_overall = lax.psum(offset_parts, ("ctx", "dp"))
+    roots_spread = lambda in_array: lax.all_gather(in_array, ("ctx", "dp")).sum(axis=0)
+    offset_overall = roots_spread(offset_parts)
     bias_scaled = offset_overall / math.sqrt(lax.axis_size("dp") * shard_length * ctx_size)
     query_grad = query_flat.astype(jnp.bfloat16)[None, None]
     key_grad = key_flattened.astype(jnp.bfloat16)[None, None]

time: 1050 us -> 868 us (0.83)
  the two profiles are of different devices: /device:TPU:128 before, /device:TPU:27 now
where the time goes in v1:
time: 868 us; the launch traced here: 865 us
  waiting for transfers between devices  573 us (66%)
  matrix products  76.2 us (9%)
  local copies, waits for them, and re-layouts  59.4 us (7%)
  blocking collectives  57.4 us (7%)
  starting transfers between devices  56.5 us (7%)
  other arithmetic  23.8 us (3%)
  between operations  14.2 us (2%)
    all_gather x1, waiting for transfers between devices, body(): lax.all_gather(in_array, ('ctx', 'dp')).sum(axis=0)  359 us
    all_to_all x1, blocking collectives, body(): lax.all_to_all(content_derivative, 'ctx', split_axis=0, concat_axis=1, ti...  57.4 us
    ppermute x1, waiting for transfers between devices, passed_along(): return lax.ppermute(value, axis, pairs)  53.1 us
    all_to_all x1, waiting for transfers between devices, body(): lax.all_to_all(asker_derivative, 'ctx', split_axis=0, concat_axis=1, tile...  45.4 us
    all_to_all x1, waiting for transfers between devices, body(): lax.all_to_all(lookup_derivative, 'ctx', split_axis=0, concat_axis=1, til...  44.2 us
    all_to_all x1, waiting for transfers between devices, body(): lax.all_to_all(key_widened, 'ctx', split_axis=1, concat_axis=0, tiled=True)  25.7 us
    all_to_all x1, waiting for transfers between devices, body(): lax.all_to_all(cot_tok, 'ctx', split_axis=1, concat_axis=0, tiled=True)  22.9 us
    all_to_all x1, waiting for transfers between devices, body(): lax.all_to_all(query_tok, 'ctx', split_axis=1, concat_axis=0, tiled=True)  22.1 us
  transfers between devices with their start and end apart: 8, of which 7 were waited for; matrix products, arithmetic and copies ran while one was open for 3% of the time, Pallas kernels for 0%

profile of v1, /device:TPU:27, one launch (start us, length us, event | category | flops | bytes accessed | tf_op | source)
XLA Modules:
  0.0 865.0 jit_solution(17443677443313876487)
XLA Ops:
  9.4 9.6 %all-to-all-start.1 = ((bf16[128,32,128]{2,0,1:T(8,128)(2,1)}), bf16[128,32,128]{2,0,1:T(8,128)(2,1)S(1)}, u32[]{:S(2)}, u32[]{:S(2)}) async-start(bf16[128,32,128]{2,0,1:T(8,128)(2,1)} %bitcast.9), calls=%async_computation.1 | async-start | bytes 2097152 | tf_op jit(solution)/shard_map/all_to_all | solution.py:113
  19.0 25.7 %all-to-all-done.1 = bf16[128,32,128]{2,0,1:T(8,128)(2,1)S(1)} async-done(((bf16[128,32,128]{2,0,1:T(8,128)(2,1)}), bf16[128,32,128]{2,0,1:T(8,128)(2,1)S(1)}, u32[]{:S(2)}, u32[]{:S(2)}) %all-to-all-start.1) | async-done | bytes 1048608 | tf_op jit(solution)/shard_map/all_to_all | solution.py:113
  45.9 6.8 all-to-all-start.3
  52.7 9.8 %collective-permute-start = (bf16[1,1,128,4096]{3,2,1,0:T(8,128)(2,1)}, bf16[1,1,128,4096]{3,2,1,0:T(8,128)(2,1)S(1)}, u32[]{:S(2)}, u32[]{:S(2)}) collective-permute-start(bf16[1,1,128,4096]{3,2,1,0:T(8,128)(2,1)} %param.10), channel_id=1, source_target_pairs={{0,384},{128,0},{256,128},{384,256},{1,385},{129,1},{257,129},{385... | collective-permute-start | bytes 3145736 | tf_op jit(solution)/shard_map/ppermute | solution.py:16
  62.4 53.1 %collective-permute-done = bf16[1,1,128,4096]{3,2,1,0:T(8,128)(2,1)S(1)} collective-permute-done((bf16[1,1,128,4096]{3,2,1,0:T(8,128)(2,1)}, bf16[1,1,128,4096]{3,2,1,0:T(8,128)(2,1)S(1)}, u32[]{:S(2)}, u32[]{:S(2)}) %collective-permute-start) | collective-permute-done | bytes 1048608 | tf_op jit(solution)/shard_map/ppermute | solution.py:16
  116.9 7.5 all-to-all-start.2
  127.3 22.9 %all-to-all-done.2 = bf16[128,32,128]{0,2,1:T(8,128)(2,1)S(1)} async-done(((bf16[128,32,128]{0,2,1:T(8,128)(2,1)}), bf16[128,32,128]{0,2,1:T(8,128)(2,1)S(1)}, u32[]{:S(2)}, u32[]{:S(2)}) %all-to-all-start.2) | async-done | bytes 1048608 | tf_op jit(solution)/shard_map/all_to_all | solution.py:115
  150.1 7.4 all-to-all-start
  161.3 22.1 %all-to-all-done = bf16[128,32,128]{2,0,1:T(8,128)(2,1)} async-done(((bf16[128,32,128]{2,0,1:T(8,128)(2,1)}), bf16[128,32,128]{2,0,1:T(8,128)(2,1)}, u32[]{:S(2)}, u32[]{:S(2)}) %all-to-all-start) | async-done | bytes 1048608 | tf_op jit(solution)/shard_map/all_to_all | solution.py:112
  187.0 126.4 %while.25 = (s32[]{:T(128)}, f32[4608,128]{1,0:T(8,128)}, f32[4608,128]{1,0:T(8,128)}, f32[8,1,512,128]{3,2,1,0:T(8,128)}, s32[8]{0:T(128)}, /*index=5*/s32[4096...) while((s32[]{:T(128)}, f32[4608,128]{1,0:T(8,128)}, ...), condition=%wide.region_4.5_spmd, body=%wide.region_0.4_spmd.sunk | while | flops 820444160 | bytes 22487844 | solution.py:87
  227.6 2.4 fusion.59
  259.2 2.4 fusion.59
  275.0 2.4 fusion.59
  290.9 2.4 fusion.59
  306.6 2.4 fusion.59
  313.5 3.1 slice.8
  316.6 7.4 all-to-all-start.5
  324.0 3.1 slice.9
  327.1 44.2 %all-to-all-done.5 = f32[4096,1,128]{2,1,0:T(1,128)S(1)} async-done(((f32[4096,1,128]{2,1,0:T(1,128)}), f32[4096,1,128]{2,1,0:T(1,128)S(1)}, u32[]{:S(2)}, u32[]{:S(2)}) %all-to-all-start.5) | async-done | bytes 2097184 | tf_op jit(solution)/shard_map/all_to_all | solution.py:137
  371.3 57.4 %all_to_all.105 = f32[4096,1,128]{2,1,0:T(1,128)} all-to-all(f32[4096,1,128]{2,1,0:T(1,128)} %bitcast.109), channel_id=1, replica_groups=mesh['pipe'=4,'ctx'=32,'dp'=4] {'ctx'}, dimensions={0} | all-to-all | bytes 4194304 | tf_op jit(solution)/shard_map/all_to_all | solution.py:138
  428.7 8.1 all-to-all-start.4
  438.7 45.4 %all-to-all-done.4 = f32[4096,1,128]{2,1,0:T(1,128)} async-done(((f32[4096,1,128]{2,1,0:T(1,128)}), f32[4096,1,128]{2,1,0:T(1,128)}, u32[]{:S(2)}, u32[]{:S(2)}) %all-to-all-start.4) | async-done | bytes 2097184 | tf_op jit(solution)/shard_map/all_to_all | solution.py:136
  495.4 359.4 %all-gather.3.cloned.1.call-done = f32[655360]{0:T(1024)} async-done(((f32[5120]{0:T(1024)}), f32[655360]{0:T(1024)}) %all-gather.3.cloned.1.call-update) | async-done | bytes 2621456 | tf_op jit(solution)/shard_map/all_gather | solution.py:154
  854.9 2.5 reshape.145
  (157 shorter events, 138.5 us)
Async XLA Ops:
  7.2 11.8 %copy-start = (bf16[1,1,128,512]{3,2,1,0:T(8,128)(2,1)S(1)}, bf16[1,1,128,512]{3,2,1,0:T(8,128)(2,1)}, u32[]{:S(2)}) copy-start(bf16[1,1,128,512]{3,2,1,0:T(8,128)(2,1)} %param.9) | copy-start | bytes 393220
  9.4 35.3 %all-to-all-start.1 = ((bf16[128,32,128]{2,0,1:T(8,128)(2,1)}), bf16[128,32,128]{2,0,1:T(8,128)(2,1)S(1)}, u32[]{:S(2)}, u32[]{:S(2)}) async-start(bf16[128,32,128]{2,0,1:T(8,128)(2,1)} %bitcast.9), calls=%async_computation.1 | async-start | bytes 2097152 | tf_op jit(solution)/shard_map/all_to_all | solution.py:113
  45.9 71.0 %all-to-all-start.3 = ((bf16[128,32,128]{2,0,1:T(8,128)(2,1)}), bf16[128,32,128]{2,0,1:T(8,128)(2,1)S(1)}, u32[]{:S(2)}, u32[]{:S(2)}) async-start(bf16[128,32,128]{2,0,1:T(8,128)(2,1)} %bitcast.17), calls=%async_computation.3 | async-start | bytes 2097152 | tf_op jit(solution)/shard_map/all_to_all | solution.py:114
  52.7 62.9 %collective-permute-start = (bf16[1,1,128,4096]{3,2,1,0:T(8,128)(2,1)}, bf16[1,1,128,4096]{3,2,1,0:T(8,128)(2,1)S(1)}, u32[]{:S(2)}, u32[]{:S(2)}) collective-permute-start(bf16[1,1,128,4096]{3,2,1,0:T(8,128)(2,1)} %param.10), channel_id=1, source_target_pairs={{0,384},{128,0},{256,128},{384,256},{1,385},{129,1},{257,129},{385... | collective-permute-start | bytes 3145736 | tf_op jit(solution)/shard_map/ppermute | solution.py:16
  116.9 33.2 %all-to-all-start.2 = ((bf16[128,32,128]{0,2,1:T(8,128)(2,1)}), bf16[128,32,128]{0,2,1:T(8,128)(2,1)S(1)}, u32[]{:S(2)}, u32[]{:S(2)}) async-start(bf16[128,32,128]{0,2,1:T(8,128)(2,1)} %bitcast.112), calls=%async_computation.2 | async-start | bytes 2097152 | tf_op jit(solution)/shard_map/all_to_all | solution.py:115
  125.9 31.7 %copy-start.1 = (s32[1,4096]{1,0:T(1,128)S(1)}, s32[1,4096]{1,0:T(1,128)}, u32[]{:S(2)}) copy-start(s32[1,4096]{1,0:T(1,128)} %param.11) | copy-start | bytes 49156
  150.1 33.3 %all-to-all-start = ((bf16[128,32,128]{2,0,1:T(8,128)(2,1)}), bf16[128,32,128]{2,0,1:T(8,128)(2,1)}, u32[]{:S(2)}, u32[]{:S(2)}) async-start(bf16[128,32,128]{2,0,1:T(8,128)(2,1)} %copy.41), calls=%async_computation | async-start | bytes 2097152 | tf_op jit(solution)/shard_map/all_to_all | solution.py:112
  316.6 54.7 %all-to-all-start.5 = ((f32[4096,1,128]{2,1,0:T(1,128)}), f32[4096,1,128]{2,1,0:T(1,128)S(1)}, u32[]{:S(2)}, u32[]{:S(2)}) async-start(f32[4096,1,128]{2,1,0:T(1,128)} %bitcast.108), calls=%async_computation.5 | async-start | bytes 4194304 | tf_op jit(solution)/shard_map/all_to_all | solution.py:137
  428.7 55.4 %all-to-all-start.4 = ((f32[4096,1,128]{2,1,0:T(1,128)}), f32[4096,1,128]{2,1,0:T(1,128)}, u32[]{:S(2)}, u32[]{:S(2)}) async-start(f32[4096,1,128]{2,1,0:T(1,128)} %bitcast.116), calls=%async_computation.4 | async-start | bytes 4194304 | tf_op jit(solution)/shard_map/all_to_all | solution.py:136
  436.7 418.1 %all-gather.3.cloned.1.call-start = ((), (), s32[]{:S(2)}) async-start(), calls=%async_computation.7 | async-start | bytes 2641920 | tf_op jit(solution)/shard_map/all_gather | solution.py:154
Sparse Core Ops, SparseCore 0:
  486.6 368.2 all-gather.2
